TPU v7x, 256 devices: a whole 4x4x8 slice. The times are simulated.
256 devices in a mesh: chan: 64 (over z, y_hi, x), win: 4 (over y_lo, core).
Axes of the slice: x: 4, y: 4 (y_hi: 2, y_lo: 2; y = y_hi * 2 + y_lo), z: 8, core: 2. Of those that a mesh axis runs over, the one named last changes fastest.
Arguments:
- traces: float32 [8, 2048, 2048], P('win', 'chan'), may hold values from -200 to 200
- quality: int32 [8, 2048], P('win', 'chan'), may hold values 0 or 1
Outputs:
- correlations: bfloat16 [2048, 2048, 128], P('chan', 'win')
Inputs may be any that keep to these rules, and one draw needn't show every extreme that they name: `quality`: 1 marks a usable window of a channel.
All inputs are finite; a program needn't handle non-finite values. No bound on the sum of `quality` on one device may be relied on, other than what follows from the above.
Results may differ from a plain program's by a relative error of at most 0.008.
Values may be sent and summed in bfloat16 or wider, within the bound.
No kernel may reach another device: no remote copies, remote signals or barrier semaphores. Data moves between devices by JAX's collectives and lax.ppermute only.
A program may use at most 128 MiB of HBM per device.

v0:
```python
import math

import jax
import jax.numpy as jnp
from jax import lax
from jax.sharding import PartitionSpec as P

SEGS = 8
NFFT = 256
F = 128
BAND = 8
LAGS = 128


epsilon = 1e-06
column_block = 512


def forward_table():
    sample_index = jnp.arange(NFFT, dtype=jnp.int32)[:, None]
    bin_index = jnp.arange(1, F + 1, dtype=jnp.int32)[None, :]
    angles = 2.0 * jnp.pi / NFFT * (sample_index * bin_index % NFFT).astype(jnp.float32)
    norm_scale = 1.0 / math.sqrt(NFFT)
    return jnp.concatenate([jnp.cos(angles), -jnp.sin(angles)], axis=1) * norm_scale


def lag_kernel(window_total):
    bin_index = jnp.arange(1, F + 1, dtype=jnp.int32)[:, None]
    lag_shift = jnp.arange(LAGS, dtype=jnp.int32)[None, :] - LAGS // 2
    angles = 2.0 * jnp.pi / NFFT * (bin_index * lag_shift % NFFT).astype(jnp.float32)
    norm_scale = 2.0 / math.sqrt(F * SEGS * window_total)
    return jnp.stack([jnp.cos(angles) * norm_scale, -jnp.sin(angles) * norm_scale]).astype(
        jnp.bfloat16
    )


def whiten(traces, quality):
    win_count, channels = (traces.shape[0], traces.shape[1])
    segments = traces.reshape(win_count, channels, SEGS, NFFT)
    spectrum = jnp.dot(segments, forward_table(), precision=lax.Precision.HIGHEST)
    real_part = spectrum[..., :F]
    imag_part = spectrum[..., F:]
    power_sum = (real_part * real_part + imag_part * imag_part).reshape(
        win_count, channels, SEGS, F // BAND, BAND
    )
    amplitude = jnp.sqrt(jnp.mean(power_sum, axis=(2, 4)) + epsilon)
    factor = quality.astype(jnp.float32)[:, :, None] / amplitude
    factor = jnp.repeat(factor, BAND, axis=2)[:, :, None, :]
    stacked_parts = jnp.stack([real_part * factor, imag_part * factor], axis=0)
    stacked_parts = jnp.transpose(stacked_parts, (2, 0, 1, 3, 4)).reshape(
        channels, 2 * win_count * SEGS, F
    )
    return stacked_parts.astype(jnp.bfloat16)


def rotate(spectra):
    middle = spectra.shape[1] // 2
    return jnp.concatenate([spectra[:, middle:], -spectra[:, :middle]], axis=1)


def block_lags(stacked, theirs, kernel):
    cross_part = jnp.einsum(
        "iwk,jwk->ijk", stacked, theirs, preferred_element_type=jnp.float32
    ).astype(jnp.bfloat16)
    cross_part = cross_part.reshape(2, stacked.shape[0] // 2, theirs.shape[0], cross_part.shape[-1])
    return jnp.einsum("pijk,pkt->jit", cross_part, kernel, preferred_element_type=jnp.float32)


def pair_lags(stacked, theirs, kernel):
    columns = theirs.shape[0]
    pieces = theirs.reshape(columns // column_block, column_block, theirs.shape[1], theirs.shape[2])
    lag_tiles = lax.map(lambda column_piece: block_lags(stacked, column_piece, kernel), pieces)
    return lag_tiles.reshape(columns, lag_tiles.shape[2], lag_tiles.shape[3])


def body(traces, quality):
    kernel = lag_kernel(lax.axis_size("win") * traces.shape[0])
    spectra = whiten(traces, quality)
    stacked = jnp.concatenate([spectra, rotate(spectra)], axis=0)
    partial_terms = pair_lags(stacked, lax.all_gather(spectra, "chan", axis=0, tiled=True), kernel)
    summed = lax.psum_scatter(
        partial_terms.astype(jnp.bfloat16), "win", scatter_dimension=0, tiled=True
    )
    return jnp.transpose(summed, (1, 0, 2))


def solution(mesh):
    in_specs = (P("win", "chan", None), P("win", "chan"))
    out_specs = P("chan", "win", None)
    return jax.shard_map(body, mesh=mesh, in_specs=in_specs, out_specs=out_specs, check_vma=False)
```

profile of v0, /device:TPU:1, one launch (start us, length us, event | category | flops | bytes accessed | tf_op | source)
XLA Modules:
  0.0 500.2 jit_solution(7143574307228338175)
XLA Ops:
  6.5 0.0 all-gather.2.cloned.1.call-start
  6.5 0.5 fusion.24
  7.1 1.7 convolution_bitcast_fusion
  8.8 0.1 copy.20
  8.9 0.7 convert_element_type.45
  9.7 0.1 copy.21
  9.7 0.1 fusion.15
  9.8 0.8 copy.22
  10.6 0.0 all-gather.2.cloned.1.call-update
  10.7 0.0 reduce-scatter.2.cloned.1.call-start
  10.7 1.0 fusion.27
  11.7 1.0 maximum_maximum_fusion
  12.7 1.7 copy.27
  14.4 0.3 multiply_convert_fusion.3
  14.8 198.2 %all-gather.2.cloned.1.call-done = bf16[2048,32,128]{2,1,0:T(8,128)(2,1)} async-done(((bf16[32,32,128]{2,1,0:T(8,128)(2,1)}), bf16[2048,32,128]{2,1,0:T(8,128)(2,1)}) %all-gather.2.cloned.1.call-update) | async-done | bytes 16777232 | tf_op jit(solution)/shard_map/all_gather | solution.py:80
  212.9 119.6 %while.10 = (s32[]{:T(128)}, bf16[4,512,32,128]{3,1,2,0:T(8,128)(2,1)}, bf16[4,512,32,128]{3,2,1,0:T(8,128)(2,1)}, bf16[64,32,128]{0,1,2:T(8,128)(2,1)S(1)}, bf16[2,128,128]{2,1,0:T(8,128)(2,1)S(1)}, /*index=5*/s32[]{:T(128)}) while((s32[]{:T(128)}, bf16[4,512,32,128]{3,1,2,0:T(8,128)(2,1)}, bf16[4,512,32,128]{3,2,1,0:T(8,128)(2,1)}, ...), condition=%wide.region_3.4_spmd, body=%wide.region_2.3_spmd.sunk | while | flops 1346371584 | bytes 46727752 | solution.py:72
  212.9 4.9 constant_dynamic-slice_fusion.2
  217.9 8.6 %copy.44 = bf16[1,512,32,128]{1,2,3,0:T(8,128)(2,1)} copy(bf16[1,512,32,128]{3,2,1,0:T(8,128)(2,1)} %constant_dynamic-slice_fusion.2) | data formatting | bytes 8388608 | tf_op jit(solution)/shard_map/while/body/jit(dynamic_index_in_dim)/dynamic_slice | solution.py:72
  226.4 4.6 convolution_convert_fusion.2
  231.0 11.8 %bitcast_dynamic-update-slice_fusion.2 = bf16[4,512,32,128]{3,1,2,0:T(8,128)(2,1)} fusion(bf16[4,512,32,128]{3,1,2,0:T(8,128)(2,1)} %get-tuple-element.101, s32[]{:T(128)} %get-tuple-element.100, bf16[2,32,512,128]{2,1,0,3:T(8,128)(2,1)S(1)} %bitcast.52, bf16[2,128,128]{2,1,0:T(8,128)(2,1)S(1)} %get-tuple-element.110), kind=kOutput, calls=%fused_computation.clone.1 | convolution fusion | flops 1073741824 | bytes 16843264 | tf_op jit(solution)/shard_map/while/body/eval_jaxpr/pijk,pkt->jit/dot_general | solution.py:66
  242.8 4.9 constant_dynamic-slice_fusion.2
  247.8 8.6 %copy.44 = bf16[1,512,32,128]{1,2,3,0:T(8,128)(2,1)} copy(bf16[1,512,32,128]{3,2,1,0:T(8,128)(2,1)} %constant_dynamic-slice_fusion.2) | data formatting | bytes 8388608 | tf_op jit(solution)/shard_map/while/body/jit(dynamic_index_in_dim)/dynamic_slice | solution.py:72
  256.3 4.6 convolution_convert_fusion.2
  260.9 11.8 %bitcast_dynamic-update-slice_fusion.2 = bf16[4,512,32,128]{3,1,2,0:T(8,128)(2,1)} fusion(bf16[4,512,32,128]{3,1,2,0:T(8,128)(2,1)} %get-tuple-element.101, s32[]{:T(128)} %get-tuple-element.100, bf16[2,32,512,128]{2,1,0,3:T(8,128)(2,1)S(1)} %bitcast.52, bf16[2,128,128]{2,1,0:T(8,128)(2,1)S(1)} %get-tuple-element.110), kind=kOutput, calls=%fused_computation.clone.1 | convolution fusion | flops 1073741824 | bytes 16843264 | tf_op jit(solution)/shard_map/while/body/eval_jaxpr/pijk,pkt->jit/dot_general | solution.py:66
  272.8 4.9 constant_dynamic-slice_fusion.2
  277.7 8.6 %copy.44 = bf16[1,512,32,128]{1,2,3,0:T(8,128)(2,1)} copy(bf16[1,512,32,128]{3,2,1,0:T(8,128)(2,1)} %constant_dynamic-slice_fusion.2) | data formatting | bytes 8388608 | tf_op jit(solution)/shard_map/while/body/jit(dynamic_index_in_dim)/dynamic_slice | solution.py:72
  286.3 4.6 convolution_convert_fusion.2
  290.8 11.8 %bitcast_dynamic-update-slice_fusion.2 = bf16[4,512,32,128]{3,1,2,0:T(8,128)(2,1)} fusion(bf16[4,512,32,128]{3,1,2,0:T(8,128)(2,1)} %get-tuple-element.101, s32[]{:T(128)} %get-tuple-element.100, bf16[2,32,512,128]{2,1,0,3:T(8,128)(2,1)S(1)} %bitcast.52, bf16[2,128,128]{2,1,0:T(8,128)(2,1)S(1)} %get-tuple-element.110), kind=kOutput, calls=%fused_computation.clone.1 | convolution fusion | flops 1073741824 | bytes 16843264 | tf_op jit(solution)/shard_map/while/body/eval_jaxpr/pijk,pkt->jit/dot_general | solution.py:66
  302.7 4.9 constant_dynamic-slice_fusion.2
  307.6 8.6 %copy.44 = bf16[1,512,32,128]{1,2,3,0:T(8,128)(2,1)} copy(bf16[1,512,32,128]{3,2,1,0:T(8,128)(2,1)} %constant_dynamic-slice_fusion.2) | data formatting | bytes 8388608 | tf_op jit(solution)/shard_map/while/body/jit(dynamic_index_in_dim)/dynamic_slice | solution.py:72
  316.2 4.6 convolution_convert_fusion.2
  320.7 11.8 %bitcast_dynamic-update-slice_fusion.2 = bf16[4,512,32,128]{3,1,2,0:T(8,128)(2,1)} fusion(bf16[4,512,32,128]{3,1,2,0:T(8,128)(2,1)} %get-tuple-element.101, s32[]{:T(128)} %get-tuple-element.100, bf16[2,32,512,128]{2,1,0,3:T(8,128)(2,1)S(1)} %bitcast.52, bf16[2,128,128]{2,1,0:T(8,128)(2,1)S(1)} %get-tuple-element.110), kind=kOutput, calls=%fused_computation.clone.1 | convolution fusion | flops 1073741824 | bytes 16843264 | tf_op jit(solution)/shard_map/while/body/eval_jaxpr/pijk,pkt->jit/dot_general | solution.py:66
  332.6 13.9 %copy.28 = bf16[4,512,32,128]{3,1,0,2:T(8,128)(2,1)} copy(bf16[4,512,32,128]{3,1,2,0:T(8,128)(2,1)} %get-tuple-element.32) | data formatting | bytes 33554432 | tf_op jit(solution)/shard_map/convert_element_type | solution.py:82
  346.5 0.0 reduce-scatter.2.cloned.1.call-update
  346.5 146.9 %reduce-scatter.2.cloned.1.call-done = bf16[512,32,128]{2,0,1:T(8,128)(2,1)} async-done(((bf16[2048,32,128]{2,0,1:T(8,128)(2,1)}), bf16[512,32,128]{2,0,1:T(8,128)(2,1)}) %reduce-scatter.2.cloned.1.call-update) | async-done | bytes 4194320 | tf_op jit(solution)/shard_map/reduce_scatter | solution.py:81
  (8 shorter events, 0.1 us)
Async XLA Ops:
  6.5 206.4 %all-gather.2.cloned.1.call-start = ((), (), s32[]{:S(2)}) async-start(), calls=%async_computation.1 | async-start | bytes 17039360 | tf_op jit(solution)/shard_map/all_gather | solution.py:80
  10.7 482.7 %reduce-scatter.2.cloned.1.call-start = ((), (), s32[]{:S(2)}) async-start(), calls=%async_computation.2 | async-start | bytes 20971520 | tf_op jit(solution)/shard_map/reduce_scatter | solution.py:81
Sparse Core Ops, SparseCore 0:
  11.0 201.9 all-gather.1
  346.6 146.7 reduce-scatter.1
where the time goes:
time: 501 us; the launch traced here: 500 us
  waiting for transfers between devices  345 us (69%)
  local copies, waits for them, and re-layouts  70.6 us (14%)
  matrix products  67.3 us (13%)
  between operations  13.5 us (3%)
    all_gather x1, waiting for transfers between devices, body(): lax.all_gather(spectra, 'chan', axis=0, tiled=True)  198 us
    reduce_scatter x1, waiting for transfers between devices, body(): lax.psum_scatter(partial_terms.astype(jnp.bfloat16), 'win', scatter_dimen...  147 us
    dynamic_slice x8, local copies, waits for them, and re-layouts, pair_lags(): lax.map(lambda column_piece: block_lags(stacked, column_piece, kernel), p...  54 us
    dot_general x4, matrix products, block_lags(): jnp.einsum('pijk,pkt->jit', cross_part, kernel, preferred_element_type=jn...  47.3 us
    dot_general x4, matrix products, block_lags(): jnp.einsum('iwk,jwk->ijk', stacked, theirs, preferred_element_type=jnp.fl...  18.3 us
    convert_element_type x1, local copies, waits for them, and re-layouts, body(): partial_terms.astype(jnp.bfloat16)  13.9 us
  transfers between devices with their start and end apart: 2, of which 2 were waited for; matrix products, arithmetic and copies ran while one was open for 1% of the time, Pallas kernels for 0%

commit v1 on v0

--- a/solution.py
+++ b/solution.py
@@ -13,7 +13,6 @@
 
 
 epsilon = 1e-06
-column_block = 512
 
 
 def forward_table():
@@ -53,35 +52,39 @@
     return stacked_parts.astype(jnp.bfloat16)
 
 
-def rotate(spectra):
-    middle = spectra.shape[1] // 2
-    return jnp.concatenate([spectra[:, middle:], -spectra[:, :middle]], axis=1)
-
-
-def block_lags(stacked, theirs, kernel):
-    cross_part = jnp.einsum(
-        "iwk,jwk->ijk", stacked, theirs, preferred_element_type=jnp.float32
-    ).astype(jnp.bfloat16)
-    cross_part = cross_part.reshape(2, stacked.shape[0] // 2, theirs.shape[0], cross_part.shape[-1])
-    return jnp.einsum("pijk,pkt->jit", cross_part, kernel, preferred_element_type=jnp.float32)
-
-
-def pair_lags(stacked, theirs, kernel):
-    columns = theirs.shape[0]
-    pieces = theirs.reshape(columns // column_block, column_block, theirs.shape[1], theirs.shape[2])
-    lag_tiles = lax.map(lambda column_piece: block_lags(stacked, column_piece, kernel), pieces)
-    return lag_tiles.reshape(columns, lag_tiles.shape[2], lag_tiles.shape[3])
+def column_permutation(n_chan, n_win):
+    per = n_chan // n_win
+    return [
+        (c * n_win + g, (per * g + c % per) * n_win + c // per)
+        for c in range(n_chan)
+        for g in range(n_win)
+    ]
 
 
 def body(traces, quality):
-    kernel = lag_kernel(lax.axis_size("win") * traces.shape[0])
+    n_chan = lax.axis_size("chan")
+    n_win = lax.axis_size("win")
+    per = n_chan // n_win
+    kernel = lag_kernel(n_win * traces.shape[0])
     spectra = whiten(traces, quality)
-    stacked = jnp.concatenate([spectra, rotate(spectra)], axis=0)
-    partial_terms = pair_lags(stacked, lax.all_gather(spectra, "chan", axis=0, tiled=True), kernel)
-    summed = lax.psum_scatter(
-        partial_terms.astype(jnp.bfloat16), "win", scatter_dimension=0, tiled=True
-    )
-    return jnp.transpose(summed, (1, 0, 2))
+    channels, parts, bins = spectra.shape
+    half = parts // 2
+
+    own = lax.all_gather(spectra, "win", axis=1, tiled=False)
+    rotated = jnp.concatenate([own[:, :, half:], -own[:, :, :half]], axis=2)
+    stacked = jnp.concatenate([own, rotated], axis=0).reshape(2 * channels, n_win * parts, bins)
+
+    piece = lax.ppermute(spectra, ("chan", "win"), column_permutation(n_chan, n_win))
+    theirs = lax.all_gather(piece, "chan", axis=0, tiled=False)
+    theirs = theirs.reshape(n_win, per, channels, parts, bins)
+    theirs = jnp.transpose(theirs, (1, 2, 0, 3, 4)).reshape(per * channels, n_win * parts, bins)
+
+    cross = jnp.einsum(
+        "iak,jak->ijk", stacked, theirs, preferred_element_type=jnp.float32
+    ).astype(jnp.bfloat16)
+    cross = cross.reshape(2, channels, cross.shape[1], bins)
+    lags = jnp.einsum("pijk,pkt->ijt", cross, kernel, preferred_element_type=jnp.float32)
+    return lags.astype(jnp.bfloat16)
 
 
 def solution(mesh):

time: 501 us -> 315 us (0.63)
  waiting for transfers between devices: 345 us -> 218 us
  matrix products: 67.3 us -> 28.3 us
  local copies, waits for them, and re-layouts: 70.6 us -> 42.2 us
  starting transfers between devices: 0.04 us -> 6.32 us
    reduce_scatter x1 -> x0, waiting for transfers between devices: 147 us -> none  [body(): lax.psum_scatter(partial_terms.astype(jnp.bfloat16), 'win', scatter_dimen...]
    dynamic_slice x8 -> x0, local copies, waits for them, and re-layouts: 54 us -> none  [pair_lags(): lax.map(lambda column_piece: block_lags(stacked, column_piece, kernel), p...]
    dot_general x8 -> x2, matrix products: 65.6 us -> 26.6 us  [the longest x1 15.2 us: body(): jnp.einsum('pijk,pkt->ijt', cross, kernel, preferred_element_type=jnp.flo...]
    reshape x0 -> x2, local copies, waits for them, and re-layouts: none -> 24.9 us  [the longest x1 21.7 us: body(): jnp.transpose(theirs, (1, 2, 0, 3, 4))]
    transpose x0 -> x1, local copies, waits for them, and re-layouts: none -> 15.5 us  [body(): jnp.transpose(theirs, (1, 2, 0, 3, 4))]
    convert_element_type x1 -> x0, local copies, waits for them, and re-layouts: 13.9 us -> none  [body(): partial_terms.astype(jnp.bfloat16)]
    all_gather x1 -> x2, waiting for transfers between devices: 198 us -> 210 us  [the longest x1 198 us: body(): theirs = lax.all_gather(piece, 'chan', axis=0, tiled=False)]
    ppermute x0 -> x1, waiting for transfers between devices: none -> 7.69 us  [body(): lax.ppermute(spectra, ('chan', 'win'), column_permutation(n_chan, n_win))]
  transfers between devices with their start and end apart: 2 -> 3, of which waited for: 2 -> 3; matrix products, arithmetic and copies ran while one was open for 1% -> 3% of each run, Pallas kernels for 0% -> 0%
where the time goes in v1:
time: 315 us; the launch traced here: 314 us
  waiting for transfers between devices  218 us (69%)
  local copies, waits for them, and re-layouts  42.2 us (13%)
  matrix products  28.3 us (9%)
  between operations  13.5 us (4%)
  starting transfers between devices  6.32 us (2%)
  other arithmetic  6.21 us (2%)
    all_gather x1, waiting for transfers between devices, body(): theirs = lax.all_gather(piece, 'chan', axis=0, tiled=False)  198 us
    reshape x1, local copies, waits for them, and re-layouts, body(): jnp.transpose(theirs, (1, 2, 0, 3, 4))  21.7 us
    transpose x1, local copies, waits for them, and re-layouts, body(): jnp.transpose(theirs, (1, 2, 0, 3, 4))  15.5 us
    dot_general x1, matrix products, body(): jnp.einsum('pijk,pkt->ijt', cross, kernel, preferred_element_type=jnp.flo...  15.2 us
    all_gather x1, waiting for transfers between devices, body(): own = lax.all_gather(spectra, 'win', axis=1, tiled=False)  12.4 us
    dot_general x1, matrix products, body(): jnp.einsum('iak,jak->ijk', stacked, theirs, preferred_element_type=jnp.fl...  11.4 us
    ppermute x1, waiting for transfers between devices, body(): lax.ppermute(spectra, ('chan', 'win'), column_permutation(n_chan, n_win))  7.69 us
  transfers between devices with their start and end apart: 3, of which 3 were waited for; matrix products, arithmetic and copies ran while one was open for 3% of the time, Pallas kernels for 0%

profile of v1, /device:TPU:1, one launch (start us, length us, event | category | flops | bytes accessed | tf_op | source)
XLA Modules:
  0.0 314.2 jit_solution(2669902719719755803)
XLA Ops:
  6.5 0.0 all-gather.4.cloned.1.call-start
  6.5 0.5 fusion.22
  7.1 1.7 convolution_bitcast_fusion
  8.8 0.1 copy.22
  8.9 0.7 convert_element_type.55
  9.7 0.1 copy.23
  9.7 0.1 multiply_bitcast_fusion.1
  9.8 0.8 copy.26
  10.6 0.0 all-gather.4.cloned.1.call-update
  10.7 0.0 all-gather.6.cloned.1.call-start
  10.7 0.1 copy.24
  10.8 6.3 %collective-permute-start = (bf16[32,32,128]{2,1,0:T(8,128)(2,1)S(1)}, bf16[32,32,128]{2,1,0:T(8,128)(2,1)S(1)}, u32[]{:S(2)}, u32[]{:S(2)}) collective-permute-start(bf16[32,32,128]{2,1,0:T(8,128)(2,1)S(1)} %copy.24), channel_id=1, source_target_pairs={{0,0},{1,64},{2,128},{3,192},{4,4},{5,68},{6,132},{7,196},{8,8},{9... | collective-permute-start | bytes 786440 | tf_op jit(solution)/shard_map/ppermute | solution.py:77
  17.1 7.7 %collective-permute-done = bf16[32,32,128]{2,1,0:T(8,128)(2,1)S(1)} collective-permute-done((bf16[32,32,128]{2,1,0:T(8,128)(2,1)S(1)}, bf16[32,32,128]{2,1,0:T(8,128)(2,1)S(1)}, u32[]{:S(2)}, u32[]{:S(2)}) %collective-permute-start) | collective-permute-done | bytes 262176 | tf_op jit(solution)/shard_map/ppermute | solution.py:77
  24.8 0.0 copy-start
  24.8 0.7 copy-done
  25.5 0.0 all-gather.6.cloned.1.call-update
  25.5 0.3 multiply_convert_fusion.1
  25.9 12.4 %all-gather.4.cloned.1.call-done = bf16[32,4,32,128]{3,2,1,0:T(8,128)(2,1)} async-done(((bf16[32,1,32,128]{3,2,1,0:T(8,128)(2,1)}), bf16[32,4,32,128]{3,2,1,0:T(8,128)(2,1)}) %all-gather.4.cloned.1.call-update) | async-done | bytes 1048592 | tf_op jit(solution)/shard_map/all_gather | solution.py:73
  38.3 1.3 fusion.26
  39.6 3.2 %maximum_maximum_fusion = bf16[64,4,32,128]{3,2,1,0:T(8,128)(2,1)} fusion(bf16[32,4,16,128]{3,2,1,0:T(8,128)(2,1)S(1)} %get-tuple-element.6, bf16[32,4,16,128]{3,2,1,0:T(8,128)(2,1)S(1)} %get-tuple-element.5, bf16[32,4,32,128]{3,2,1,0:T(8,128)(2,1)} %all-gather.4.cloned.1.call-done), kind=kLoop, calls=%fused_computation.4 | loop fusion | flops 6291456 | bytes 4194304 | tf_op jit(solution)/shard_map/concatenate | solution.py:75
  42.7 3.3 %copy.28 = bf16[64,128,128]{1,0,2:T(8,128)(2,1)S(1)} copy(bf16[64,128,128]{2,1,0:T(8,128)(2,1)} %bitcast.43) | data formatting | bytes 4194304 | tf_op jit(solution)/shard_map/reshape | solution.py:75
  46.0 197.6 %all-gather.6.cloned.1.call-done = bf16[2048,32,128]{2,1,0:T(8,128)(2,1)} async-done(((bf16[32,32,128]{2,1,0:T(8,128)(2,1)}), bf16[2048,32,128]{2,1,0:T(8,128)(2,1)}) %all-gather.6.cloned.1.call-update) | async-done | bytes 16777232 | tf_op jit(solution)/shard_map/all_gather | solution.py:78
  243.6 15.5 %copy.25 = bf16[16,32,4,32,128]{4,3,2,1,0:T(8,128)(2,1)} copy(bf16[16,32,4,32,128]{4,3,1,0,2:T(8,128)(2,1)} %bitcast.42) | data formatting | bytes 33554432 | tf_op jit(solution)/shard_map/transpose | solution.py:80
  259.1 21.7 %copy.27 = bf16[512,128,128]{1,0,2:T(8,128)(2,1)} copy(bf16[512,128,128]{2,1,0:T(8,128)(2,1)} %bitcast.40) | data formatting | bytes 33554432 | tf_op jit(solution)/shard_map/reshape | solution.py:80
  280.8 11.4 %convolution_convert_fusion = bf16[128,512,64]{1,2,0:T(8,128)(2,1)} fusion(bf16[512,128,128]{1,0,2:T(8,128)(2,1)} %copy.27, bf16[64,128,128]{1,0,2:T(8,128)(2,1)S(1)} %copy.28), kind=kOutput, calls=%fused_computation.3 | convolution fusion | flops 1077936128 | bytes 27262976 | tf_op jit(solution)/shard_map/iak,jak->ijk/dot_general | solution.py:82
  292.2 15.2 %bitcast_convert_fusion = bf16[32,512,128]{2,1,0:T(8,128)(2,1)} fusion(bf16[2,32,512,128]{2,1,0,3:T(8,128)(2,1)} %bitcast.41, bf16[1,128,128]{2,1,0:T(8,128)(2,1)S(1)} %get-tuple-element.10, bf16[1,128,128]{2,1,0:T(8,128)(2,1)S(1)} %get-tuple-element.9), kind=kOutput, calls=%fused_computation | convolution fusion | flops 1075871744 | bytes 12648448 | tf_op jit(solution)/shard_map/pijk,pkt->ijt/dot_general | solution.py:86
  (6 shorter events, 0.1 us)
Async XLA Ops:
  6.5 31.8 %all-gather.4.cloned.1.call-start = ((), (), s32[]{:S(2)}) async-start(), calls=%async_computation | async-start | bytes 1310720 | tf_op jit(solution)/shard_map/all_gather | solution.py:73
  10.7 233.0 %all-gather.6.cloned.1.call-start = ((), (), s32[]{:S(2)}) async-start(), calls=%async_computation.1 | async-start | bytes 17039360 | tf_op jit(solution)/shard_map/all_gather | solution.py:78
  10.8 14.0 %collective-permute-start = (bf16[32,32,128]{2,1,0:T(8,128)(2,1)S(1)}, bf16[32,32,128]{2,1,0:T(8,128)(2,1)S(1)}, u32[]{:S(2)}, u32[]{:S(2)}) collective-permute-start(bf16[32,32,128]{2,1,0:T(8,128)(2,1)S(1)} %copy.24), channel_id=1, source_target_pairs={{0,0},{1,64},{2,128},{3,192},{4,4},{5,68},{6,132},{7,196},{8,8},{9... | collective-permute-start | bytes 786440 | tf_op jit(solution)/shard_map/ppermute | solution.py:77
  24.8 0.7 copy-start
Sparse Core Ops, SparseCore 0:
  10.8 27.4 all-gather.3
  41.9 201.6 all-gather.5

commit v2 on v1

--- a/solution.py
+++ b/solution.py
@@ -61,6 +61,9 @@
     ]
 
 
+CHUNKS = 4
+
+
 def body(traces, quality):
     n_chan = lax.axis_size("chan")
     n_win = lax.axis_size("win")
@@ -70,21 +73,31 @@
     channels, parts, bins = spectra.shape
     half = parts // 2
 
-    own = lax.all_gather(spectra, "win", axis=1, tiled=False)
+    piece = lax.ppermute(spectra, ("chan", "win"), column_permutation(n_chan, n_win))
+
+    received = [spectra] + [
+        lax.ppermute(spectra, "win", [(s, (s + shift) % n_win) for s in range(n_win)])
+        for shift in range(1, n_win)
+    ]
+    mirrored = [received[(-m) % n_win] for m in range(n_win)]
+    doubled = jnp.stack(mirrored + mirrored, axis=1)
+    own = lax.dynamic_slice_in_dim(doubled, n_win - lax.axis_index("win"), n_win, axis=1)
     rotated = jnp.concatenate([own[:, :, half:], -own[:, :, :half]], axis=2)
     stacked = jnp.concatenate([own, rotated], axis=0).reshape(2 * channels, n_win * parts, bins)
 
-    piece = lax.ppermute(spectra, ("chan", "win"), column_permutation(n_chan, n_win))
-    theirs = lax.all_gather(piece, "chan", axis=0, tiled=False)
-    theirs = theirs.reshape(n_win, per, channels, parts, bins)
-    theirs = jnp.transpose(theirs, (1, 2, 0, 3, 4)).reshape(per * channels, n_win * parts, bins)
-
-    cross = jnp.einsum(
-        "iak,jak->ijk", stacked, theirs, preferred_element_type=jnp.float32
-    ).astype(jnp.bfloat16)
-    cross = cross.reshape(2, channels, cross.shape[1], bins)
-    lags = jnp.einsum("pijk,pkt->ijt", cross, kernel, preferred_element_type=jnp.float32)
-    return lags.astype(jnp.bfloat16)
+    size = channels // CHUNKS
+    outs = []
+    for q in range(CHUNKS):
+        theirs = lax.all_gather(piece[q * size:(q + 1) * size], "chan", axis=0, tiled=False)
+        theirs = theirs.reshape(n_win, per, size, parts, bins)
+        theirs = jnp.transpose(theirs, (1, 2, 0, 3, 4)).reshape(per * size, n_win * parts, bins)
+        cross = jnp.einsum(
+            "iak,jak->ijk", stacked, theirs, preferred_element_type=jnp.float32
+        ).astype(jnp.bfloat16)
+        cross = cross.reshape(2, channels, per * size, bins)
+        lags = jnp.einsum("pijk,pkt->ijt", cross, kernel, preferred_element_type=jnp.float32)
+        outs.append(lags.astype(jnp.bfloat16).reshape(channels, per, size, LAGS))
+    return jnp.stack(outs, axis=2).reshape(channels, per * channels, LAGS)
 
 
 def solution(mesh):

time: 315 us -> 573 us (1.82)
  waiting for transfers between devices: 218 us -> 448 us
  local copies, waits for them, and re-layouts: 42.2 us -> 56.7 us
  starting transfers between devices: 6.32 us -> 16.8 us
    all_gather x2 -> x4, waiting for transfers between devices: 210 us -> 430 us  [body(): lax.all_gather(piece[q * size:(q + 1) * size], 'chan', axis=0, tiled=False)]
    ppermute x0 -> x3, starting transfers between devices: none -> 10.4 us  [body(): lax.ppermute(spectra, 'win', [(s, (s + shift) % n_win) for s in range(n_w...]
    ppermute x0 -> x3, waiting for transfers between devices: none -> 8.78 us  [body(): lax.ppermute(spectra, 'win', [(s, (s + shift) % n_win) for s in range(n_w...]
    transpose x1 -> x4, local copies, waits for them, and re-layouts: 15.5 us -> 22.2 us  [body(): jnp.transpose(theirs, (1, 2, 0, 3, 4))]
    reshape x1 -> x4, local copies, waits for them, and re-layouts: 21.7 us -> 26.9 us  [body(): jnp.transpose(theirs, (1, 2, 0, 3, 4))]
    dot_general x1 -> x4, matrix products: 11.4 us -> 16.5 us  [body(): jnp.einsum('iak,jak->ijk', stacked, theirs, preferred_element_type=jnp.fl...]
    dot_general x1 -> x4, matrix products: 15.2 us -> 12.4 us  [body(): jnp.einsum('pijk,pkt->ijt', cross, kernel, preferred_element_type=jnp.flo...]
  transfers between devices with their start and end apart: 3 -> 8, of which waited for: 3 -> 7; matrix products, arithmetic and copies ran while one was open for 3% -> 11% of each run, Pallas kernels for 0% -> 0%
where the time goes in v2:
time: 573 us; the launch traced here: 569 us
  waiting for transfers between devices  448 us (78%)
  local copies, waits for them, and re-layouts  56.7 us (10%)
  matrix products  30.6 us (5%)
  starting transfers between devices  16.8 us (3%)
  between operations  13.4 us (2%)
    all_gather x4, waiting for transfers between devices, body(): lax.all_gather(piece[q * size:(q + 1) * size], 'chan', axis=0, tiled=False)  430 us
    reshape x4, local copies, waits for them, and re-layouts, body(): jnp.transpose(theirs, (1, 2, 0, 3, 4))  26.9 us
    transpose x4, local copies, waits for them, and re-layouts, body(): jnp.transpose(theirs, (1, 2, 0, 3, 4))  22.2 us
    dot_general x4, matrix products, body(): jnp.einsum('iak,jak->ijk', stacked, theirs, preferred_element_type=jnp.fl...  16.5 us
    dot_general x4, matrix products, body(): jnp.einsum('pijk,pkt->ijt', cross, kernel, preferred_element_type=jnp.flo...  12.4 us
  transfers between devices with their start and end apart: 8, of which 7 were waited for; matrix products, arithmetic and copies ran while one was open for 11% of the time, Pallas kernels for 0%

profile of v2, /device:TPU:1, one launch (start us, length us, event | category | flops | bytes accessed | tf_op | source)
XLA Modules:
  0.0 569.4 jit_solution(14083788584774780449)
XLA Ops:
  6.5 0.5 fusion.44
  7.1 1.6 convolution_bitcast_fusion
  8.8 0.1 copy.60
  9.0 0.1 copy.61
  9.1 0.1 multiply_bitcast_fusion.1
  9.2 0.1 copy.62
  9.3 6.3 %collective-permute-start = (bf16[32,32,128]{2,1,0:T(8,128)(2,1)S(1)}, bf16[32,32,128]{2,1,0:T(8,128)(2,1)S(1)}, u32[]{:S(2)}, u32[]{:S(2)}) collective-permute-start(bf16[32,32,128]{2,1,0:T(8,128)(2,1)S(1)} %copy.62), channel_id=1, source_target_pairs={{0,0},{1,64},{2,128},{3,192},{4,4},{5,68},{6,132},{7,196},{8,8},{9... | collective-permute-start | bytes 786440 | tf_op jit(solution)/shard_map/ppermute | solution.py:76
  15.6 7.7 %collective-permute-done = bf16[32,32,128]{2,1,0:T(8,128)(2,1)S(1)} collective-permute-done((bf16[32,32,128]{2,1,0:T(8,128)(2,1)S(1)}, bf16[32,32,128]{2,1,0:T(8,128)(2,1)S(1)}, u32[]{:S(2)}, u32[]{:S(2)}) %collective-permute-start) | collective-permute-done | bytes 262176 | tf_op jit(solution)/shard_map/ppermute | solution.py:76
  23.2 0.7 fusion.47
  24.0 0.0 all-gather.11.cloned.1.call-start
  24.0 0.7 all-gather.11.cloned.1.call-update
  24.7 0.0 all-gather.13.cloned.1.call-start
  24.8 0.7 all-gather.13.cloned.1.call-update
  25.5 0.5 all-gather.15.cloned.1.call-update
  26.0 0.1 collective-permute-start.1
  26.1 8.4 %collective-permute-start.2 = (bf16[32,32,128]{2,1,0:T(8,128)(2,1)S(1)}, bf16[32,32,128]{2,1,0:T(8,128)(2,1)S(1)}, u32[]{:S(2)}, u32[]{:S(2)}) collective-permute-start(bf16[32,32,128]{2,1,0:T(8,128)(2,1)S(1)} %copy.62), channel_id=1, source_target_pairs={{0,2},{1,3},{2,0},{3,1},{4,6},{5,7},{6,4},{7,5},{8,10},{9,11},{10,... | collective-permute-start | bytes 786440 | tf_op jit(solution)/shard_map/ppermute | solution.py:79
  34.5 1.9 collective-permute-start.3
  36.4 0.1 copy_dynamic-update-slice_fusion
  36.5 0.3 multiply_convert_fusion.1
  36.9 3.2 collective-permute-done.2
  40.2 5.6 collective-permute-done.3
  45.8 0.1 copy_dynamic-update-slice_fusion.1
  46.0 0.1 constant_dynamic-slice_fusion.1
  46.2 0.3 constant_dynamic-slice_fusion
  46.4 1.8 maximum_maximum_fusion
  48.2 3.3 copy.70
  51.5 104.8 %all-gather.9.cloned.1.call-done = bf16[512,32,128]{2,1,0:T(8,128)(2,1)} async-done(((bf16[8,32,128]{2,1,0:T(8,128)(2,1)}), bf16[512,32,128]{2,1,0:T(8,128)(2,1)}) %all-gather.9.cloned.1.call-update) | async-done | bytes 4194320 | tf_op jit(solution)/shard_map/all_gather | solution.py:91
  156.3 5.5 copy.63
  161.8 6.7 %copy.69 = bf16[128,128,128]{1,0,2:T(8,128)(2,1)} copy(bf16[128,128,128]{2,1,0:T(8,128)(2,1)} %bitcast.105) | data formatting | bytes 8388608 | tf_op jit(solution)/shard_map/reshape | solution.py:93
  168.5 115.6 %all-gather.11.cloned.1.call-done = bf16[512,32,128]{2,1,0:T(8,128)(2,1)} async-done(((bf16[8,32,128]{2,1,0:T(8,128)(2,1)}), bf16[512,32,128]{2,1,0:T(8,128)(2,1)}) %all-gather.11.cloned.1.call-update) | async-done | bytes 4194320 | tf_op jit(solution)/shard_map/all_gather | solution.py:91
  284.0 5.5 copy.72
  289.5 6.8 %copy.73 = bf16[128,128,128]{1,0,2:T(8,128)(2,1)} copy(bf16[128,128,128]{2,1,0:T(8,128)(2,1)} %bitcast.106) | data formatting | bytes 8388608 | tf_op jit(solution)/shard_map/reshape | solution.py:93
  296.3 115.5 %all-gather.13.cloned.1.call-done = bf16[512,32,128]{2,1,0:T(8,128)(2,1)} async-done(((bf16[8,32,128]{2,1,0:T(8,128)(2,1)}), bf16[512,32,128]{2,1,0:T(8,128)(2,1)}) %all-gather.13.cloned.1.call-update) | async-done | bytes 4194320 | tf_op jit(solution)/shard_map/all_gather | solution.py:91
  411.7 5.5 copy.76
  417.2 6.7 %copy.77 = bf16[128,128,128]{1,0,2:T(8,128)(2,1)} copy(bf16[128,128,128]{2,1,0:T(8,128)(2,1)} %bitcast.107) | data formatting | bytes 8388608 | tf_op jit(solution)/shard_map/reshape | solution.py:93
  424.0 5.3 convolution_convert_fusion.3
  429.3 2.6 fusion.16
  431.9 3.0 convolution_convert_fusion.2
  434.9 3.7 fusion.19
  438.6 3.0 convolution_convert_fusion.1
  441.6 3.6 fusion.22
  445.2 94.1 %all-gather.15.cloned.1.call-done = bf16[512,32,128]{2,1,0:T(8,128)(2,1)} async-done(((bf16[8,32,128]{2,1,0:T(8,128)(2,1)}), bf16[512,32,128]{2,1,0:T(8,128)(2,1)}) %all-gather.15.cloned.1.call-update) | async-done | bytes 4194320 | tf_op jit(solution)/shard_map/all_gather | solution.py:91
  539.3 5.7 %copy.80 = bf16[16,8,4,32,128]{4,3,2,1,0:T(8,128)(2,1)} copy(bf16[16,8,4,32,128]{4,3,1,0,2:T(8,128)(2,1)} %bitcast.114) | data formatting | bytes 8388608 | tf_op jit(solution)/shard_map/transpose | solution.py:93
  545.0 6.7 %copy.81 = bf16[128,128,128]{1,0,2:T(8,128)(2,1)} copy(bf16[128,128,128]{2,1,0:T(8,128)(2,1)} %bitcast.108) | data formatting | bytes 8388608 | tf_op jit(solution)/shard_map/reshape | solution.py:93
  551.7 5.2 convolution_convert_fusion
  556.9 2.6 fusion.25
  559.5 0.6 pad_maximum_fusion
  560.1 2.8 copy.84
  (27 shorter events, 0.4 us)
Async XLA Ops:
  6.5 2.4 copy-start.4
  6.5 149.8 %all-gather.9.cloned.1.call-start = ((), (), s32[]{:S(2)}) async-start(), calls=%async_computation | async-start | bytes 4259840 | tf_op jit(solution)/shard_map/all_gather | solution.py:91
  9.3 14.0 %collective-permute-start = (bf16[32,32,128]{2,1,0:T(8,128)(2,1)S(1)}, bf16[32,32,128]{2,1,0:T(8,128)(2,1)S(1)}, u32[]{:S(2)}, u32[]{:S(2)}) collective-permute-start(bf16[32,32,128]{2,1,0:T(8,128)(2,1)S(1)} %copy.62), channel_id=1, source_target_pairs={{0,0},{1,64},{2,128},{3,192},{4,4},{5,68},{6,132},{7,196},{8,8},{9... | collective-permute-start | bytes 786440 | tf_op jit(solution)/shard_map/ppermute | solution.py:76
  24.0 260.0 %all-gather.11.cloned.1.call-start = ((), (), s32[]{:S(2)}) async-start(), calls=%async_computation.1 | async-start | bytes 4259840 | tf_op jit(solution)/shard_map/all_gather | solution.py:91
  24.7 387.0 %all-gather.13.cloned.1.call-start = ((), (), s32[]{:S(2)}) async-start(), calls=%async_computation.2 | async-start | bytes 4259840 | tf_op jit(solution)/shard_map/all_gather | solution.py:91
  25.4 513.9 %all-gather.15.cloned.1.call-start = ((), (), s32[]{:S(2)}) async-start(), calls=%async_computation.3 | async-start | bytes 4259840 | tf_op jit(solution)/shard_map/all_gather | solution.py:91
  26.0 10.8 %collective-permute-start.1 = (bf16[32,32,128]{2,1,0:T(8,128)(2,1)S(1)}, bf16[32,32,128]{2,1,0:T(8,128)(2,1)S(1)}, u32[]{:S(2)}, u32[]{:S(2)}) collective-permute-start(bf16[32,32,128]{2,1,0:T(8,128)(2,1)S(1)} %copy.62), channel_id=1, source_target_pairs={{0,3},{1,0},{2,1},{3,2},{4,7},{5,4},{6,5},{7,6},{8,11},{9,8},{10,9... | collective-permute-start | bytes 786440 | tf_op jit(solution)/shard_map/ppermute | solution.py:79
  26.1 14.0 %collective-permute-start.2 = (bf16[32,32,128]{2,1,0:T(8,128)(2,1)S(1)}, bf16[32,32,128]{2,1,0:T(8,128)(2,1)S(1)}, u32[]{:S(2)}, u32[]{:S(2)}) collective-permute-start(bf16[32,32,128]{2,1,0:T(8,128)(2,1)S(1)} %copy.62), channel_id=1, source_target_pairs={{0,2},{1,3},{2,0},{3,1},{4,6},{5,7},{6,4},{7,5},{8,10},{9,11},{10,... | collective-permute-start | bytes 786440 | tf_op jit(solution)/shard_map/ppermute | solution.py:79
  34.5 11.3 %collective-permute-start.3 = (bf16[32,32,128]{2,1,0:T(8,128)(2,1)S(1)}, bf16[32,32,128]{2,1,0:T(8,128)(2,1)S(1)}, u32[]{:S(2)}, u32[]{:S(2)}) collective-permute-start(bf16[32,32,128]{2,1,0:T(8,128)(2,1)S(1)} %copy.62), channel_id=1, source_target_pairs={{0,1},{1,2},{2,3},{3,0},{4,5},{5,6},{6,7},{7,4},{8,9},{9,10},{10,1... | collective-permute-start | bytes 786440 | tf_op jit(solution)/shard_map/ppermute | solution.py:79
  424.0 7.9 %copy-start = (bf16[128,128,128]{1,0,2:T(8,128)(2,1)S(1)}, bf16[128,128,128]{1,0,2:T(8,128)(2,1)}, u32[]{:S(2)}) copy-start(bf16[128,128,128]{1,0,2:T(8,128)(2,1)} %copy.73) | copy-start | bytes 12582916
  431.9 6.7 %copy-start.1 = (bf16[128,128,128]{1,0,2:T(8,128)(2,1)S(1)}, bf16[128,128,128]{1,0,2:T(8,128)(2,1)}, u32[]{:S(2)}) copy-start(bf16[128,128,128]{1,0,2:T(8,128)(2,1)} %copy.77) | copy-start | bytes 12582916
  556.9 2.6 copy-start.2
  556.9 2.6 copy-start.3
Sparse Core Ops, SparseCore 0:
  24.1 132.1 all-gather.8
  159.9 124.0 all-gather.10
  287.6 124.0 all-gather.12
  415.2 124.0 all-gather.14

commit v3 on v2

--- a/solution.py
+++ b/solution.py
@@ -61,7 +61,7 @@
     ]
 
 
-CHUNKS = 4
+CHUNKS = 1
 
 
 def body(traces, quality):

time: 573 us -> 303 us (0.53)
  waiting for transfers between devices: 448 us -> 198 us
  local copies, waits for them, and re-layouts: 56.7 us -> 42.6 us
    all_gather x4 -> x1, waiting for transfers between devices: 430 us -> 181 us  [body(): lax.all_gather(piece[q * size:(q + 1) * size], 'chan', axis=0, tiled=False)]
    transpose x4 -> x1, local copies, waits for them, and re-layouts: 22.2 us -> 15.5 us  [body(): jnp.transpose(theirs, (1, 2, 0, 3, 4))]
    reshape x4 -> x1, local copies, waits for them, and re-layouts: 26.9 us -> 21.6 us  [body(): jnp.transpose(theirs, (1, 2, 0, 3, 4))]
    dot_general x4 -> x1, matrix products: 16.5 us -> 11.4 us  [body(): jnp.einsum('iak,jak->ijk', stacked, theirs, preferred_element_type=jnp.fl...]
    dot_general x4 -> x1, matrix products: 12.4 us -> 15.2 us  [body(): jnp.einsum('pijk,pkt->ijt', cross, kernel, preferred_element_type=jnp.flo...]
  transfers between devices with their start and end apart: 8 -> 5, of which waited for: 7 -> 4; matrix products, arithmetic and copies ran while one was open for 11% -> 2% of each run, Pallas kernels for 0% -> 0%
where the time goes in v3:
time: 303 us; the launch traced here: 302 us
  waiting for transfers between devices  198 us (65%)
  local copies, waits for them, and re-layouts  42.6 us (14%)
  matrix products  28.3 us (9%)
  starting transfers between devices  16.7 us (6%)
  between operations  13.6 us (4%)
  other arithmetic  3.14 us (1%)
    all_gather x1, waiting for transfers between devices, body(): lax.all_gather(piece[q * size:(q + 1) * size], 'chan', axis=0, tiled=False)  181 us
    reshape x1, local copies, waits for them, and re-layouts, body(): jnp.transpose(theirs, (1, 2, 0, 3, 4))  21.6 us
    transpose x1, local copies, waits for them, and re-layouts, body(): jnp.transpose(theirs, (1, 2, 0, 3, 4))  15.5 us
    dot_general x1, matrix products, body(): jnp.einsum('pijk,pkt->ijt', cross, kernel, preferred_element_type=jnp.flo...  15.2 us
    dot_general x1, matrix products, body(): jnp.einsum('iak,jak->ijk', stacked, theirs, preferred_element_type=jnp.fl...  11.4 us
    ppermute x3, starting transfers between devices, body(): lax.ppermute(spectra, 'win', [(s, (s + shift) % n_win) for s in range(n_w...  10.5 us
    ppermute x3, waiting for transfers between devices, body(): lax.ppermute(spectra, 'win', [(s, (s + shift) % n_win) for s in range(n_w...  9.1 us
    ppermute x1, waiting for transfers between devices, body(): lax.ppermute(spectra, ('chan', 'win'), column_permutation(n_chan, n_win))  7.88 us
  transfers between devices with their start and end apart: 5, of which 4 were waited for; matrix products, arithmetic and copies ran while one was open for 2% of the time, Pallas kernels for 0%

profile of v3, /device:TPU:1, one launch (start us, length us, event | category | flops | bytes accessed | tf_op | source)
XLA Modules:
  0.0 302.1 jit_solution(3462625953436784632)
XLA Ops:
  6.5 0.0 copy-start.1
  6.5 0.0 all-gather.3.cloned.1.call-start
  6.5 0.5 fusion.22
  7.1 1.6 convolution_bitcast_fusion
  8.8 0.1 copy.30
  8.9 0.0 copy-done.1
  9.0 0.1 copy.31
  9.1 0.1 multiply_bitcast_fusion.1
  9.2 0.8 copy.32
  10.0 6.3 %collective-permute-start = (bf16[32,32,128]{2,1,0:T(8,128)(2,1)}, bf16[32,32,128]{2,1,0:T(8,128)(2,1)S(1)}, u32[]{:S(2)}, u32[]{:S(2)}) collective-permute-start(bf16[32,32,128]{2,1,0:T(8,128)(2,1)} %copy.32), channel_id=1, source_target_pairs={{0,0},{1,64},{2,128},{3,192},{4,4},{5,68},{6,132},{7,196},{8,8},{9... | collective-permute-start | bytes 786440 | tf_op jit(solution)/shard_map/ppermute | solution.py:76
  16.2 7.9 %collective-permute-done = bf16[32,32,128]{2,1,0:T(8,128)(2,1)S(1)} collective-permute-done((bf16[32,32,128]{2,1,0:T(8,128)(2,1)}, bf16[32,32,128]{2,1,0:T(8,128)(2,1)S(1)}, u32[]{:S(2)}, u32[]{:S(2)}) %collective-permute-start) | collective-permute-done | bytes 262176 | tf_op jit(solution)/shard_map/ppermute | solution.py:76
  24.1 0.0 copy-start
  24.1 0.7 copy-done
  24.8 0.0 all-gather.3.cloned.1.call-update
  24.8 0.1 collective-permute-start.1
  24.9 8.5 %collective-permute-start.2 = (bf16[32,32,128]{2,1,0:T(8,128)(2,1)}, bf16[32,32,128]{2,1,0:T(8,128)(2,1)S(1)}, u32[]{:S(2)}, u32[]{:S(2)}) collective-permute-start(bf16[32,32,128]{2,1,0:T(8,128)(2,1)} %copy.32), channel_id=1, source_target_pairs={{0,2},{1,3},{2,0},{3,1},{4,6},{5,7},{6,4},{7,5},{8,10},{9,11},{10,... | collective-permute-start | bytes 786440 | tf_op jit(solution)/shard_map/ppermute | solution.py:79
  33.4 1.9 collective-permute-start.3
  35.3 0.1 copy_dynamic-update-slice_fusion
  35.4 0.3 multiply_convert_fusion.1
  35.8 0.0 collective-permute-done.1
  35.8 3.5 %collective-permute-done.2 = bf16[32,32,128]{2,1,0:T(8,128)(2,1)S(1)} collective-permute-done((bf16[32,32,128]{2,1,0:T(8,128)(2,1)}, bf16[32,32,128]{2,1,0:T(8,128)(2,1)S(1)}, u32[]{:S(2)}, u32[]{:S(2)}) %collective-permute-start.2) | collective-permute-done | bytes 262176 | tf_op jit(solution)/shard_map/ppermute | solution.py:79
  39.4 5.6 %collective-permute-done.3 = bf16[32,32,128]{2,1,0:T(8,128)(2,1)S(1)} collective-permute-done((bf16[32,32,128]{2,1,0:T(8,128)(2,1)}, bf16[32,32,128]{2,1,0:T(8,128)(2,1)S(1)}, u32[]{:S(2)}, u32[]{:S(2)}) %collective-permute-start.3) | collective-permute-done | bytes 262176 | tf_op jit(solution)/shard_map/ppermute | solution.py:79
  45.0 0.1 copy_dynamic-update-slice_fusion.1
  45.3 0.1 constant_dynamic-slice_fusion.1
  45.4 0.3 constant_dynamic-slice_fusion
  45.7 1.8 maximum_maximum_fusion
  47.5 3.3 %copy.40 = bf16[64,128,128]{1,0,2:T(8,128)(2,1)S(1)} copy(bf16[64,128,128]{2,1,0:T(8,128)(2,1)} %bitcast.52) | data formatting | bytes 4194304 | tf_op jit(solution)/shard_map/reshape | solution.py:86
  50.8 180.8 %all-gather.3.cloned.1.call-done = bf16[2048,32,128]{2,1,0:T(8,128)(2,1)} async-done(((bf16[32,32,128]{2,1,0:T(8,128)(2,1)}), bf16[2048,32,128]{2,1,0:T(8,128)(2,1)}) %all-gather.3.cloned.1.call-update) | async-done | bytes 16777232 | tf_op jit(solution)/shard_map/all_gather | solution.py:91
  231.6 15.5 %copy.33 = bf16[16,32,4,32,128]{4,3,2,1,0:T(8,128)(2,1)} copy(bf16[16,32,4,32,128]{4,3,1,0,2:T(8,128)(2,1)} %bitcast.51) | data formatting | bytes 33554432 | tf_op jit(solution)/shard_map/transpose | solution.py:93
  247.1 21.6 %copy.39 = bf16[512,128,128]{1,0,2:T(8,128)(2,1)} copy(bf16[512,128,128]{2,1,0:T(8,128)(2,1)} %bitcast.49) | data formatting | bytes 33554432 | tf_op jit(solution)/shard_map/reshape | solution.py:93
  268.7 11.4 %convolution_convert_fusion = bf16[128,512,64]{1,2,0:T(8,128)(2,1)} fusion(bf16[512,128,128]{1,0,2:T(8,128)(2,1)} %copy.39, bf16[64,128,128]{1,0,2:T(8,128)(2,1)S(1)} %copy.40), kind=kOutput, calls=%fused_computation.3 | convolution fusion | flops 1077936128 | bytes 27262976 | tf_op jit(solution)/shard_map/iak,jak->ijk/dot_general | solution.py:94
  280.1 15.2 %bitcast_convert_fusion = bf16[32,512,128]{2,1,0:T(8,128)(2,1)} fusion(bf16[2,32,512,128]{2,1,0,3:T(8,128)(2,1)} %bitcast.50, bf16[1,128,128]{2,1,0:T(8,128)(2,1)S(1)} %get-tuple-element.10, bf16[1,128,128]{2,1,0:T(8,128)(2,1)S(1)} %get-tuple-element.9), kind=kOutput, calls=%fused_computation | convolution fusion | flops 1075871744 | bytes 12648448 | tf_op jit(solution)/shard_map/pijk,pkt->ijt/dot_general | solution.py:98
  (13 shorter events, 0.3 us)
Async XLA Ops:
  6.5 2.4 copy-start.1
  6.5 225.1 %all-gather.3.cloned.1.call-start = ((), (), s32[]{:S(2)}) async-start(), calls=%async_computation | async-start | bytes 17039360 | tf_op jit(solution)/shard_map/all_gather | solution.py:91
  10.0 14.2 %collective-permute-start = (bf16[32,32,128]{2,1,0:T(8,128)(2,1)}, bf16[32,32,128]{2,1,0:T(8,128)(2,1)S(1)}, u32[]{:S(2)}, u32[]{:S(2)}) collective-permute-start(bf16[32,32,128]{2,1,0:T(8,128)(2,1)} %copy.32), channel_id=1, source_target_pairs={{0,0},{1,64},{2,128},{3,192},{4,4},{5,68},{6,132},{7,196},{8,8},{9... | collective-permute-start | bytes 786440 | tf_op jit(solution)/shard_map/ppermute | solution.py:76
  24.1 0.7 copy-start
  24.8 10.9 %collective-permute-start.1 = (bf16[32,32,128]{2,1,0:T(8,128)(2,1)}, bf16[32,32,128]{2,1,0:T(8,128)(2,1)S(1)}, u32[]{:S(2)}, u32[]{:S(2)}) collective-permute-start(bf16[32,32,128]{2,1,0:T(8,128)(2,1)} %copy.32), channel_id=1, source_target_pairs={{0,3},{1,0},{2,1},{3,2},{4,7},{5,4},{6,5},{7,6},{8,11},{9,8},{10,9... | collective-permute-start | bytes 786440 | tf_op jit(solution)/shard_map/ppermute | solution.py:79
  24.9 14.4 %collective-permute-start.2 = (bf16[32,32,128]{2,1,0:T(8,128)(2,1)}, bf16[32,32,128]{2,1,0:T(8,128)(2,1)S(1)}, u32[]{:S(2)}, u32[]{:S(2)}) collective-permute-start(bf16[32,32,128]{2,1,0:T(8,128)(2,1)} %copy.32), channel_id=1, source_target_pairs={{0,2},{1,3},{2,0},{3,1},{4,6},{5,7},{6,4},{7,5},{8,10},{9,11},{10,... | collective-permute-start | bytes 786440 | tf_op jit(solution)/shard_map/ppermute | solution.py:79
  33.4 11.6 %collective-permute-start.3 = (bf16[32,32,128]{2,1,0:T(8,128)(2,1)}, bf16[32,32,128]{2,1,0:T(8,128)(2,1)S(1)}, u32[]{:S(2)}, u32[]{:S(2)}) collective-permute-start(bf16[32,32,128]{2,1,0:T(8,128)(2,1)} %copy.32), channel_id=1, source_target_pairs={{0,1},{1,2},{2,3},{3,0},{4,5},{5,6},{6,7},{7,4},{8,9},{9,10},{10,1... | collective-permute-start | bytes 786440 | tf_op jit(solution)/shard_map/ppermute | solution.py:79
Sparse Core Ops, SparseCore 0:
  25.0 206.6 all-gather.2
